TPU v7x, 512 devices: a whole 4x8x8 slice. The times are simulated.
512 devices in a mesh: dp: 4 (over y_hi, core), context: 16 (over y_lo, x), tensor: 8 (over z).
Axes of the slice: x: 4, y: 8 (y_hi: 2, y_lo: 4; y = y_hi * 4 + y_lo), z: 8, core: 2. Of those that a mesh axis runs over, the one named last changes fastest.
Arguments:
- queries: bfloat16 [8192, 4096], P(('dp', 'context'), 'tensor'), parts along dimension 0, may hold values from -6 to 6
- keys: bfloat16 [8192, 1024], P(('dp', 'context'), 'tensor'), parts along dimension 0, may hold values from -6 to 6
- values: bfloat16 [8192, 1024], P(('dp', 'context'), 'tensor'), parts along dimension 0, may hold values from -6 to 6
- order: int32 [8192], P('dp'), parts along dimension 0, may hold values from 0 to 2047, as said below
- out_weight: bfloat16 [4096, 4096], P('tensor', 'context'), may hold values from -0.125 to 0.125
Outputs:
- output: bfloat16 [8192, 4096], P(('dp', 'context'), 'tensor'), parts along dimension 0
There are 4 independent parts, one for each index of `dp`. A program takes and returns all parts, laid end to end along the dimension named above; an argument that names none is the same for every part. Nothing has to cross between parts.
Inputs may be any that keep to these rules, and one draw needn't show every extreme that they name: A permutation of the positions; each aligned block of 128 rows holds 128 consecutive positions in increasing order, starting at a multiple of 128.
All inputs are finite; a program needn't handle non-finite values.
Results may differ from a plain program's by a relative error of at most 0.019.
Values may be sent and summed in bfloat16 or wider, within the bound.
No kernel may reach another device: no remote copies, remote signals or barrier semaphores. Data moves between devices by JAX's collectives and lax.ppermute only.
A program may use at most 64 MiB of HBM per device.

v0:
```python
import math
import jax
import jax.numpy as jnp
from jax import lax
from jax.sharding import PartitionSpec as P

QUERY_HEADS = 32
KEY_VALUE_HEADS = 8
HEAD_SIZE = 128


def per_device(queries, keys, values, order, out_weight):
    row_count = queries.shape[0]
    local_groups = keys.shape[1] // HEAD_SIZE
    query_head_group = QUERY_HEADS // KEY_VALUE_HEADS
    score_scale = 1.0 / math.sqrt(HEAD_SIZE)
    first_row = lax.axis_index("context") * row_count
    query_pos = lax.dynamic_slice_in_dim(order, first_row, row_count, 0)
    stacked = queries.reshape(row_count, local_groups, query_head_group, HEAD_SIZE)
    stacked = stacked.transpose(1, 2, 0, 3).reshape(
        local_groups, query_head_group * row_count, HEAD_SIZE
    )
    stacked_pos = jnp.tile(query_pos, query_head_group)
    stacked_rows = query_head_group * row_count
    kv_part = lax.all_gather(jnp.concatenate([keys, values], axis=1), "context", axis=0, tiled=True)
    key_part = kv_part[:, : keys.shape[1]]
    value_part = kv_part[:, keys.shape[1] :]
    key_count = key_part.shape[0]
    running_max = jnp.full((local_groups, stacked_rows), -1e30, jnp.float32)
    key_heads = key_part.reshape(key_count, local_groups, HEAD_SIZE)
    value_heads = value_part.reshape(key_count, local_groups, HEAD_SIZE)
    scores = (
        jnp.einsum("grd,kgd->grk", stacked, key_heads, preferred_element_type=jnp.float32)
        * score_scale
    )
    visible = order[None, None, :] <= stacked_pos[None, :, None]
    scores = jnp.where(visible, scores, -1e30)
    new_max = jnp.maximum(running_max, jnp.max(scores, axis=2))
    weights = jnp.where(visible, jnp.exp(scores - new_max[..., None]), 0.0)
    new_sum = jnp.sum(weights, axis=2)
    product = jnp.einsum(
        "grk,kgd->grd",
        weights.astype(jnp.bfloat16),
        value_heads,
        preferred_element_type=jnp.float32,
    )
    attended = (product / new_sum[..., None]).astype(jnp.bfloat16)
    attended = attended.reshape(local_groups, query_head_group, row_count, HEAD_SIZE).transpose(
        2, 0, 1, 3
    )
    attended = attended.reshape(row_count, local_groups * query_head_group * HEAD_SIZE)
    partial_out = jnp.dot(
        attended,
        lax.all_gather(out_weight, "context", axis=1, tiled=True),
        preferred_element_type=jnp.float32,
    )
    return lax.psum_scatter(
        partial_out.astype(jnp.bfloat16), "tensor", scatter_dimension=1, tiled=True
    )


def solution(mesh):
    placed = (
        P(("dp", "context"), "tensor"),
        P(("dp", "context"), "tensor"),
        P(("dp", "context"), "tensor"),
        P("dp"),
        P("tensor", "context"),
    )
    return jax.shard_map(
        per_device,
        mesh=mesh,
        in_specs=placed,
        out_specs=P(("dp", "context"), "tensor"),
        check_vma=False,
    )
```

profile of v0, /device:TPU:6, one launch (start us, length us, event | category | flops | bytes accessed | tf_op | source)
XLA Modules:
  0.0 242.8 jit_solution(16070495082497380029)
XLA Ops:
  6.5 0.0 copy-start
  6.5 0.0 all-gather.3.cloned.1.call-start
  6.5 1.4 pad_maximum_fusion
  8.0 0.0 all-gather.3.cloned.1.call-update
  8.0 0.0 all-gather.5.cloned.1.call-start
  8.0 0.7 all-gather.5.cloned.1.call-update
  8.7 0.0 reduce-scatter.2.cloned.1.call-start
  8.8 1.0 copy.7
  9.8 0.1 copy.8
  10.0 0.8 dynamic_slice.3
  10.7 82.1 %all-gather.3.cloned.1.call-done = bf16[2048,256]{1,0:T(8,128)(2,1)} async-done(((bf16[128,256]{1,0:T(8,128)(2,1)}), bf16[2048,256]{1,0:T(8,128)(2,1)}) %all-gather.3.cloned.1.call-update) | async-done | bytes 1048592 | tf_op jit(solution)/shard_map/all_gather | solution.py:25
  92.9 0.0 copy-start.1
  92.9 2.0 fusion
  94.9 0.0 copy-done
  94.9 1.3 fusion.1
  96.1 0.0 copy-done.1
  96.2 1.6 fusion.8
  97.8 0.1 copy.9
  97.9 92.8 %all-gather.5.cloned.1.call-done = bf16[512,4096]{1,0:T(8,128)(2,1)} async-done(((bf16[512,256]{1,0:T(8,128)(2,1)}), bf16[512,4096]{1,0:T(8,128)(2,1)}) %all-gather.5.cloned.1.call-update) | async-done | bytes 4194320 | tf_op jit(solution)/shard_map/all_gather | solution.py:54
  190.7 3.9 %convolution_convert_fusion = bf16[128,4096]{1,0:T(8,128)(2,1)} fusion(bf16[128,512]{0,1:T(8,128)(2,1)S(1)} %bitcast.29, bf16[512,4096]{1,0:T(8,128)(2,1)} %all-gather.5.cloned.1.call-done), kind=kOutput, calls=%fused_computation.2 | convolution fusion | flops 537395200 | bytes 5373952 | tf_op jit(solution)/shard_map/dot_general | solution.py:52
  194.6 0.0 reduce-scatter.2.cloned.1.call-update
  194.6 41.6 %reduce-scatter.2.cloned.1.call-done = bf16[128,512]{1,0:T(8,128)(2,1)} async-done(((bf16[128,4096]{1,0:T(8,128)(2,1)}), bf16[128,512]{1,0:T(8,128)(2,1)}) %reduce-scatter.2.cloned.1.call-update) | async-done | bytes 131088 | tf_op jit(solution)/shard_map/reduce_scatter | solution.py:57
  (2 shorter events, 0.0 us)
Async XLA Ops:
  6.5 88.3 %copy-start = (s32[2048]{0:T(1024)S(1)}, s32[2048]{0:T(1024)}, u32[]{:S(2)}) copy-start(s32[2048]{0:T(1024)} %param.8) | copy-start | bytes 24580
  6.5 86.3 %all-gather.3.cloned.1.call-start = ((), (), s32[]{:S(2)}) async-start(), calls=%async_computation.1 | async-start | bytes 1114112 | tf_op jit(solution)/shard_map/all_gather | solution.py:25
  8.0 182.7 %all-gather.5.cloned.1.call-start = ((), (), s32[]{:S(2)}) async-start(), calls=%async_computation.2 | async-start | bytes 4456448 | tf_op jit(solution)/shard_map/all_gather | solution.py:54
  8.7 227.5 %reduce-scatter.2.cloned.1.call-start = ((), (), s32[]{:S(2)}) async-start(), calls=%async_computation.3 | async-start | bytes 1179648 | tf_op jit(solution)/shard_map/reduce_scatter | solution.py:57
  92.9 3.3 %copy-start.1 = (bf16[2048,256]{1,0:T(8,128)(2,1)S(1)}, bf16[2048,256]{1,0:T(8,128)(2,1)}, u32[]{:S(2)}) copy-start(bf16[2048,256]{1,0:T(8,128)(2,1)} %all-gather.3.cloned.1.call-done) | copy-start | bytes 3145732
Sparse Core Ops, SparseCore 0:
  9.4 83.3 all-gather.2
  94.9 95.7 all-gather.4
  194.8 41.4 reduce-scatter.1
where the time goes:
time: 243 us
  waiting for transfers between devices  217 us (89%)
  between operations  13.2 us (5%)
  matrix products  7.49 us (3%)
  other arithmetic  2.69 us (1%)
    all_gather x1, waiting for transfers between devices, per_device(): lax.all_gather(out_weight, 'context', axis=1, tiled=True)  92.8 us
    all_gather x1, waiting for transfers between devices, per_device(): lax.all_gather(jnp.concatenate([keys, values], axis=1), 'context', axis=0...  82.1 us
    reduce_scatter x1, waiting for transfers between devices, per_device(): lax.psum_scatter(partial_out.astype(jnp.bfloat16), 'tensor', scatter_dime...  41.6 us
  transfers between devices with their start and end apart: 3, of which 3 were waited for; matrix products, arithmetic and copies ran while one was open for 3% of the time, Pallas kernels for 0%

commit v1 on v0

--- a/solution.py
+++ b/solution.py
@@ -3,10 +3,23 @@
 import jax.numpy as jnp
 from jax import lax
 from jax.sharding import PartitionSpec as P
+from jax.lax import all_to_all, axis_size
 
 QUERY_HEADS = 32
 KEY_VALUE_HEADS = 8
 HEAD_SIZE = 128
+
+
+def apply_pools_over_axis(frame_in, dimension_no):
+    return jnp.concatenate(
+        all_to_all(
+            jnp.stack(axis_size("context") * [frame_in]),
+            axis_name="context",
+            split_axis=0,
+            concat_axis=0,
+        ),
+        axis=dimension_no,
+    )
 
 
 def per_device(queries, keys, values, order, out_weight):
@@ -22,7 +35,7 @@
     )
     stacked_pos = jnp.tile(query_pos, query_head_group)
     stacked_rows = query_head_group * row_count
-    kv_part = lax.all_gather(jnp.concatenate([keys, values], axis=1), "context", axis=0, tiled=True)
+    kv_part = apply_pools_over_axis(jnp.concatenate([keys, values], axis=1), 0)
     key_part = kv_part[:, : keys.shape[1]]
     value_part = kv_part[:, keys.shape[1] :]
     key_count = key_part.shape[0]

time: 243 us -> 170 us (0.70)
  waiting for transfers between devices: 217 us -> 135 us
  starting transfers between devices: 0.08 us -> 9.45 us
    all_gather x1 -> x0, waiting for transfers between devices: 82.1 us -> none  [per_device(): lax.all_gather(jnp.concatenate([keys, values], axis=1), 'context', axis=0...]
    all_gather x1, waiting for transfers between devices: 92.8 us -> 65.2 us  [per_device(): lax.all_gather(out_weight, 'context', axis=1, tiled=True)]
    all_to_all x0 -> x1, waiting for transfers between devices: none -> 23.6 us  [apply_pools_over_axis(): all_to_all(jnp.stack(axis_size('context') * [frame_in]), axis_name='conte...]
    all_to_all x0 -> x1, starting transfers between devices: none -> 9.41 us  [apply_pools_over_axis(): all_to_all(jnp.stack(axis_size('context') * [frame_in]), axis_name='conte...]
    reduce_scatter x1, waiting for transfers between devices: 41.6 us -> 45.2 us  [per_device(): lax.psum_scatter(partial_out.astype(jnp.bfloat16), 'tensor', scatter_dime...]
  transfers between devices with their start and end apart: 3 -> 3, of which waited for: 3 -> 3; matrix products, arithmetic and copies ran while one was open for 3% -> 5% of each run, Pallas kernels for 0% -> 0%
where the time goes in v1:
time: 170 us
  waiting for transfers between devices  135 us (79%)
  between operations  13.4 us (8%)
  starting transfers between devices  9.45 us (6%)
  matrix products  6.92 us (4%)
  local copies, waits for them, and re-layouts  3.13 us (2%)
  other arithmetic  2.05 us (1%)
    all_gather x1, waiting for transfers between devices, per_device(): lax.all_gather(out_weight, 'context', axis=1, tiled=True)  65.2 us
    reduce_scatter x1, waiting for transfers between devices, per_device(): lax.psum_scatter(partial_out.astype(jnp.bfloat16), 'tensor', scatter_dime...  45.2 us
    all_to_all x1, waiting for transfers between devices, apply_pools_over_axis(): all_to_all(jnp.stack(axis_size('context') * [frame_in]), axis_name='conte...  23.6 us
    all_to_all x1, starting transfers between devices, apply_pools_over_axis(): all_to_all(jnp.stack(axis_size('context') * [frame_in]), axis_name='conte...  9.41 us
    dot_general x1, matrix products, per_device(): jnp.dot(attended, lax.all_gather(out_weight, 'context', axis=1, tiled=Tru...  3.9 us
  transfers between devices with their start and end apart: 3, of which 3 were waited for; matrix products, arithmetic and copies ran while one was open for 5% of the time, Pallas kernels for 0%

profile of v1, /device:TPU:6, one launch (start us, length us, event | category | flops | bytes accessed | tf_op | source)
XLA Modules:
  0.0 169.7 jit_solution(1522206891832039284)
XLA Ops:
  6.5 0.0 all-gather.2.cloned.1.call-start
  6.5 0.7 all-gather.2.cloned.1.call-update
  7.3 0.8 pad_maximum_fusion
  8.0 1.1 stack.2
  9.1 0.0 copy-start
  9.1 9.4 %all-to-all-start = ((bf16[16,128,256]{2,1,0:T(8,128)(2,1)}), bf16[16,128,256]{2,1,0:T(8,128)(2,1)S(1)}, u32[]{:S(2)}, u32[]{:S(2)}) async-start(bf16[16,128,256]{2,1,0:T(8,128)(2,1)} %stack.2), calls=%async_computation | async-start | bytes 2097152 | tf_op jit(solution)/shard_map/all_to_all | solution.py:15
  18.5 0.0 reduce-scatter.2.cloned.1.call-start
  18.6 1.0 copy.7
  19.6 0.1 copy.8
  19.7 0.8 dynamic_slice.3
  20.5 23.6 %all-to-all-done = bf16[16,128,256]{2,1,0:T(8,128)(2,1)S(1)} async-done(((bf16[16,128,256]{2,1,0:T(8,128)(2,1)}), bf16[16,128,256]{2,1,0:T(8,128)(2,1)S(1)}, u32[]{:S(2)}, u32[]{:S(2)}) %all-to-all-start) | async-done | bytes 1048608 | tf_op jit(solution)/shard_map/all_to_all | solution.py:15
  44.1 1.4 fusion
  45.6 0.0 copy-done
  45.6 1.3 fusion.1
  46.8 1.6 fusion.8
  48.4 0.1 copy.9
  48.6 65.2 %all-gather.2.cloned.1.call-done = bf16[512,4096]{1,0:T(8,128)(2,1)} async-done(((bf16[512,256]{1,0:T(8,128)(2,1)}), bf16[512,4096]{1,0:T(8,128)(2,1)}) %all-gather.2.cloned.1.call-update) | async-done | bytes 4194320 | tf_op jit(solution)/shard_map/all_gather | solution.py:67
  113.7 3.9 %convolution_convert_fusion = bf16[128,4096]{1,0:T(8,128)(2,1)} fusion(bf16[128,512]{0,1:T(8,128)(2,1)S(1)} %bitcast.32, bf16[512,4096]{1,0:T(8,128)(2,1)} %all-gather.2.cloned.1.call-done), kind=kOutput, calls=%fused_computation.2 | convolution fusion | flops 537395200 | bytes 5373952 | tf_op jit(solution)/shard_map/dot_general | solution.py:65
  117.6 0.0 reduce-scatter.2.cloned.1.call-update
  117.7 45.2 %reduce-scatter.2.cloned.1.call-done = bf16[128,512]{1,0:T(8,128)(2,1)} async-done(((bf16[128,4096]{1,0:T(8,128)(2,1)}), bf16[128,512]{1,0:T(8,128)(2,1)}) %reduce-scatter.2.cloned.1.call-update) | async-done | bytes 131088 | tf_op jit(solution)/shard_map/reduce_scatter | solution.py:70
  (2 shorter events, 0.0 us)
Async XLA Ops:
  6.5 107.2 %all-gather.2.cloned.1.call-start = ((), (), s32[]{:S(2)}) async-start(), calls=%async_computation.2 | async-start | bytes 4456448 | tf_op jit(solution)/shard_map/all_gather | solution.py:67
  9.1 36.4 %copy-start = (s32[2048]{0:T(1024)S(1)}, s32[2048]{0:T(1024)}, u32[]{:S(2)}) copy-start(s32[2048]{0:T(1024)} %param.8) | copy-start | bytes 24580
  9.1 35.0 %all-to-all-start = ((bf16[16,128,256]{2,1,0:T(8,128)(2,1)}), bf16[16,128,256]{2,1,0:T(8,128)(2,1)S(1)}, u32[]{:S(2)}, u32[]{:S(2)}) async-start(bf16[16,128,256]{2,1,0:T(8,128)(2,1)} %stack.2), calls=%async_computation | async-start | bytes 2097152 | tf_op jit(solution)/shard_map/all_to_all | solution.py:15
  18.5 144.4 %reduce-scatter.2.cloned.1.call-start = ((), (), s32[]{:S(2)}) async-start(), calls=%async_computation.3 | async-start | bytes 1179648 | tf_op jit(solution)/shard_map/reduce_scatter | solution.py:70
Sparse Core Ops, SparseCore 0:
  9.3 104.3 all-gather.1
  117.8 45.0 reduce-scatter.1
